TPU v7x, 32 devices: a whole 2x2x4 slice. The times are simulated.
32 devices in a mesh: rep: 2 (over x), member: 4 (over y, core), tp: 4 (over z).
Axes of the slice: x: 2, y: 2, z: 4, core: 2. Of those that a mesh axis runs over, the one named last changes fastest.
Arguments:
- states: bfloat16 [4096, 1024], P(('rep', 'member', 'tp')), parts along dimension 0, may hold values from -6 to 6
- member_of: int32 [4096, 1], P(('rep', 'member', 'tp')), parts along dimension 0, may hold values from 0 to 1; in each aligned block of 128 rows (0 to 127, 128 to 255, ...) at most 128 rows name the same one
- place: int32 [4096], P(('rep', 'member', 'tp')), parts along dimension 0, may hold values from 0 to 2047, as said below
- norm_gain: float32 [2, 1024], replicated, may hold values from 0.5 to 2
- w_up: bfloat16 [4, 1024, 2048], P('member', None, 'tp'), may hold values from -0.1875 to 0.1875
- w_down: bfloat16 [4, 2048, 1024], P('member', 'tp'), may hold values from -0.09375 to 0.09375
- policy_gain: float32 [1024], replicated, may hold values from 0.5 to 2
- w_policy: bfloat16 [1024, 128], replicated, may hold values from -0.1875 to 0.1875
Outputs:
- imagined: bfloat16 [4096, 1024], P(('rep', 'member', 'tp')), parts along dimension 0
- action: bfloat16 [4096, 128], P(('rep', 'member', 'tp')), parts along dimension 0
There are 2 independent parts, one for each index of `rep`. A program takes and returns all parts, laid end to end along the dimension named above; an argument that names none is the same for every part. Nothing has to cross between parts.
Inputs may be any that keep to these rules, and one draw needn't show every extreme that they name: `member_of`: at most 128 of the rows of one device name any one member, and that count is reached on some device. `place`: A permutation of the 2048 learner positions; learner device k holds positions k * 128 to (k + 1) * 128 - 1, and the rows of each device go exactly 8 to every learner device.
All inputs are finite; a program needn't handle non-finite values.
Results may differ from a plain program's by a relative error of at most 0.0069.
Values may be sent and summed in bfloat16 or wider, within the bound.
No kernel may reach another device: no remote copies, remote signals or barrier semaphores. Data moves between devices by JAX's collectives and lax.ppermute only.
A program may use at most 128 MiB of HBM per device.

v0:
```python
import jax
import jax.numpy as jnp
from jax import lax
from jax.sharding import PartitionSpec as P

PARTIAL_DTYPE = jnp.bfloat16


def from_partner(value, axis, distance):
    return lax.ppermute(value, axis, [(i, i ^ 1 << distance) for i in range(lax.axis_size(axis))])


def from_chip_behind(value, axis, chips_back):
    size = lax.axis_size(axis)
    return lax.ppermute(value, axis, [(i, (i + 2 * chips_back) % size) for i in range(size)])


def swap_parts(value):
    n_rep = lax.axis_size("rep")
    return [value] + [
        lax.ppermute(value, "rep", [(i, (i + step) % n_rep) for i in range(n_rep)])
        for step in range(1, n_rep)
    ]


def fetch_shared(up, down, chips_back):
    n_rep = lax.axis_size("rep")
    share = up.shape[1] // n_rep
    rep_here = lax.axis_index("rep")
    got_up = from_chip_behind(
        lax.dynamic_slice_in_dim(up, rep_here * share, share, axis=1), "member", chips_back
    )
    got_up, down = lax.optimization_barrier((got_up, down))
    got_down = from_chip_behind(
        lax.dynamic_slice_in_dim(down, rep_here * share, share, axis=0), "member", chips_back
    )
    up_parts = swap_parts(got_up)
    down_parts = swap_parts(got_down)
    partner_up = [from_partner(part, "member", 0) for part in up_parts]
    partner_down = [from_partner(part, "member", 0) for part in down_parts]
    return (up_parts + partner_up, down_parts + partner_down)


def rms_scale(values, gain):
    mean_square = jnp.mean(values * values, axis=-1, keepdims=True)
    return values * lax.rsqrt(mean_square + 1e-06) * gain


def running_rank(member_hits):
    return jnp.sum((jnp.cumsum(member_hits, axis=0) - member_hits) * member_hits, axis=1)


def local(states, member_of, place, norm_gain, w_up, w_down, policy_gain, w_policy):
    n_member = lax.axis_size("member")
    n_tp = lax.axis_size("tp")
    n_dev = n_member * n_tp
    member_total = n_member // 2
    rows_here = states.shape[0]
    feature_width = states.shape[1]
    own_member = lax.axis_index("member") // 2
    own_block = (own_member, w_up[0], w_down[0])
    fetched = [
        ((own_member - back + member_total) % member_total, *fetch_shared(w_up[0], w_down[0], back))
        for back in range(1, member_total)
    ]
    per_learner = rows_here // n_dev
    learner = place // rows_here
    learner_hits = (learner[:, None] == jnp.arange(n_dev, dtype=jnp.int32)[None, :]).astype(
        jnp.int32
    )
    lane_index = learner * per_learner + running_rank(learner_hits)
    placer = jnp.arange(rows_here, dtype=jnp.int32)[:, None] == lane_index[None, :]
    states = jnp.dot(
        placer.astype(jnp.bfloat16), states, preferred_element_type=jnp.float32
    ).astype(jnp.bfloat16)
    member = jnp.sum(placer.astype(jnp.int32) * member_of[:, 0][None, :], axis=1)
    packed_spot = jnp.sum(placer.astype(jnp.int32) * (place % rows_here)[None, :], axis=1)
    gain_rows = jnp.take(norm_gain, member, axis=0)
    normed = rms_scale(states.astype(jnp.float32), gain_rows).astype(jnp.bfloat16)
    member_lanes = jnp.where(
        jnp.arange(128, dtype=jnp.int32)[None, :] == 0, member[:, None], 0
    ).astype(jnp.bfloat16)
    gathered = lax.all_gather(
        jnp.concatenate([normed, member_lanes], axis=1), "tp", axis=0, tiled=True
    )
    gathered_rows = gathered[:, :feature_width]
    gathered_member = gathered[:, feature_width].astype(jnp.int32)

    def apply_block(block_member, up_here, down_here):
        keep = (gathered_member == block_member).astype(jnp.bfloat16)[:, None]
        hidden = (
            jax.nn.gelu(jnp.dot(gathered_rows, up_here, preferred_element_type=jnp.float32)).astype(
                jnp.bfloat16
            )
            * keep
        )
        return jnp.dot(hidden, down_here, preferred_element_type=jnp.float32)

    def apply_pair(block_member, up_here, down_here):
        both_up = jnp.concatenate([up_here, from_partner(up_here, "member", 0)], axis=1)
        both_down = jnp.concatenate([down_here, from_partner(down_here, "member", 0)], axis=0)
        return apply_block(block_member, both_up, both_down)

    terms = [apply_pair(*own_block)]
    for block_member, up_here, down_here in fetched:
        terms, up_here, down_here = lax.optimization_barrier((terms, up_here, down_here))
        terms = terms + [
            apply_block(
                block_member, jnp.concatenate(up_here, axis=1), jnp.concatenate(down_here, axis=0)
            )
        ]
    tp_here = lax.axis_index("tp")
    by_target = [term.reshape(n_tp, rows_here, feature_width) for term in terms]

    def slice_for(target):
        pieces = [lax.dynamic_index_in_dim(term, target, 0, keepdims=False) for term in by_target]
        total = pieces[0]
        for piece in pieces[1:]:
            total = total + piece
        return total

    change = slice_for(tp_here)
    for shift in range(1, n_tp):
        change = change + lax.ppermute(
            slice_for((tp_here + shift) % n_tp).astype(PARTIAL_DTYPE),
            "tp",
            [(i, (i + shift) % n_tp) for i in range(n_tp)],
        ).astype(jnp.float32)
    packed = (states.astype(jnp.float32) + change).astype(jnp.bfloat16)
    spot_lanes = jnp.where(
        jnp.arange(128, dtype=jnp.int32)[None, :] == 0, packed_spot[:, None], 0
    ).astype(jnp.bfloat16)
    arrivals = lax.all_to_all(
        jnp.concatenate([packed, spot_lanes], axis=1).reshape(
            n_dev, per_learner, feature_width + 128
        ),
        ("member", "tp"),
        split_axis=0,
        concat_axis=0,
        tiled=True,
    )
    arrivals = arrivals.reshape(n_dev * per_learner, feature_width + 128)
    arrival_spots = arrivals[:, feature_width].astype(jnp.int32)
    settle = (jnp.arange(rows_here, dtype=jnp.int32)[:, None] == arrival_spots[None, :]).astype(
        jnp.bfloat16
    )
    imagined = jnp.dot(
        settle, arrivals[:, :feature_width], preferred_element_type=jnp.float32
    ).astype(jnp.bfloat16)
    policy_normed = rms_scale(imagined.astype(jnp.float32), policy_gain).astype(jnp.bfloat16)
    action = jnp.tanh(jnp.dot(policy_normed, w_policy, preferred_element_type=jnp.float32)).astype(
        jnp.bfloat16
    )
    return (imagined, action)


def solution(mesh):
    in_specs = (
        P(("rep", "member", "tp"), None),
        P(("rep", "member", "tp"), None),
        P(("rep", "member", "tp")),
        P(),
        P("member", None, "tp"),
        P("member", "tp", None),
        P(),
        P(),
    )
    out_specs = (P(("rep", "member", "tp"), None), P(("rep", "member", "tp"), None))
    return jax.shard_map(local, mesh=mesh, in_specs=in_specs, out_specs=out_specs, check_vma=False)
```

profile of v0, /device:TPU:0, one launch (start us, length us, event | category | flops | bytes accessed | tf_op | source)
XLA Modules:
  0.0 118.7 jit_solution(594228416031735746)
XLA Ops:
  7.2 0.0 copy-start
  7.2 0.0 all-gather.2.cloned.1.call-start
  7.2 0.7 and_select_fusion
  7.9 0.1 fusion.86
  8.0 0.2 reduce_window_sum.11
  8.2 0.2 select_reduce_fusion.2
  8.4 0.8 select_reduce_fusion.1
  9.2 0.3 multiply_reduce_fusion
  9.5 0.1 select_convert_fusion.1
  9.6 0.8 gather_fusion
  10.4 0.0 copy-start.3
  10.4 0.0 copy-start.2
  10.4 0.1 multiply_convert_fusion
  10.6 0.8 pad_maximum_fusion
  11.3 0.0 all-gather.2.cloned.1.call-update
  11.4 0.4 copy-done.3
  11.8 3.0 %collective-permute-start.2 = (bf16[1024,256]{1,0:T(8,128)(2,1)S(1)}, bf16[1024,256]{1,0:T(8,128)(2,1)S(1)}, u32[]{:S(2)}, u32[]{:S(2)}) collective-permute-start(bf16[1024,256]{1,0:T(8,128)(2,1)S(1)} %dynamic-slice_bitcast_fusion), channel_id=1, source_target_pairs={{0,8},{4,12},{8,0},{12,4},{1,9},{5,13},{9,1},{13,5},{2,10},{6,14},... | collective-permute-start | bytes 1572872 | tf_op jit(solution)/shard_map/ppermute | solution.py:15
  14.8 0.0 collective-permute-start.1
  14.8 11.9 %collective-permute-done.2 = bf16[1024,256]{1,0:T(8,128)(2,1)S(1)} collective-permute-done((bf16[1024,256]{1,0:T(8,128)(2,1)S(1)}, bf16[1024,256]{1,0:T(8,128)(2,1)S(1)}, u32[]{:S(2)}, u32[]{:S(2)}) %collective-permute-start.2) | collective-permute-done | bytes 524320 | tf_op jit(solution)/shard_map/ppermute | solution.py:15
  26.8 1.8 %collective-permute-start.6 = (bf16[256,1024]{1,0:T(8,128)(2,1)S(1)}, bf16[256,1024]{1,0:T(8,128)(2,1)}, u32[]{:S(2)}, u32[]{:S(2)}) collective-permute-start(bf16[256,1024]{1,0:T(8,128)(2,1)S(1)} %constant_dynamic-slice_fusion), channel_id=1, source_target_pairs={{0,8},{4,12},{8,0},{12,4},{1,9},{5,13},{9,1},{13,5},{2,10},{6,14},... | collective-permute-start | bytes 1572872 | tf_op jit(solution)/shard_map/ppermute | solution.py:15
  28.6 0.0 collective-permute-start
  28.6 1.5 %collective-permute-start.3 = (bf16[1024,256]{1,0:T(8,128)(2,1)S(1)}, bf16[1024,256]{1,0:T(8,128)(2,1)}, u32[]{:S(2)}, u32[]{:S(2)}) collective-permute-start(bf16[1024,256]{1,0:T(8,128)(2,1)S(1)} %collective-permute-done.2), channel_id=1, source_target_pairs={{0,16},{16,0},{1,17},{17,1},{2,18},{18,2},{3,19},{19,3},{4,20},{20... | collective-permute-start | bytes 1572872 | tf_op jit(solution)/shard_map/ppermute | solution.py:21
  30.1 10.1 %collective-permute-done.6 = bf16[256,1024]{1,0:T(8,128)(2,1)} collective-permute-done((bf16[256,1024]{1,0:T(8,128)(2,1)S(1)}, bf16[256,1024]{1,0:T(8,128)(2,1)}, u32[]{:S(2)}, u32[]{:S(2)}) %collective-permute-start.6) | collective-permute-done | bytes 524320 | tf_op jit(solution)/shard_map/ppermute | solution.py:15
  40.2 1.4 %collective-permute-start.7 = (bf16[256,1024]{1,0:T(8,128)(2,1)}, bf16[256,1024]{1,0:T(8,128)(2,1)}, u32[]{:S(2)}, u32[]{:S(2)}) collective-permute-start(bf16[256,1024]{1,0:T(8,128)(2,1)} %collective-permute-done.6), channel_id=1, source_target_pairs={{0,16},{16,0},{1,17},{17,1},{2,18},{18,2},{3,19},{19,3},{4,20},{20... | collective-permute-start | bytes 1572872 | tf_op jit(solution)/shard_map/ppermute | solution.py:21
  41.6 0.0 collective-permute-start.4
  41.6 3.1 %all-gather.2.cloned.1.call-done = bf16[512,1152]{1,0:T(8,128)(2,1)} async-done(((bf16[128,1152]{1,0:T(8,128)(2,1)}), bf16[512,1152]{1,0:T(8,128)(2,1)}) %all-gather.2.cloned.1.call-update) | async-done | bytes 1179664 | tf_op jit(solution)/shard_map/all_gather | solution.py:83
  44.7 1.1 fusion.84
  45.7 0.0 collective-permute-done.1
  45.8 0.1 collective-permute-start.8
  45.8 0.5 collective-permute-start.5
  46.3 7.9 %collective-permute-done.7 = bf16[256,1024]{1,0:T(8,128)(2,1)} collective-permute-done((bf16[256,1024]{1,0:T(8,128)(2,1)}, bf16[256,1024]{1,0:T(8,128)(2,1)}, u32[]{:S(2)}, u32[]{:S(2)}) %collective-permute-start.7) | collective-permute-done | bytes 524320 | tf_op jit(solution)/shard_map/ppermute | solution.py:21
  54.3 0.0 collective-permute-start.9
  54.3 0.0 collective-permute-done
  54.3 4.9 %fusion.20 = f32[512,1024]{1,0:T(8,128)S(1)} fusion(bf16[512,1024]{1,0:T(8,128)(2,1)} %collective-permute-done.1, bf16[512,1024]{1,0:T(8,128)(2,1)} %bitcast.38, bf16[1024,512]{1,0:T(8,128)(2,1)} %collective-permute-done, bf16[1024,512]{1,0:T(8,128)(2,1)} %bitcast.41, bf16[512,1152]{1,0:T(8,128)(2,1)} %all-gather.2.cloned.1.call-done, ...), kind=kOutput, calls=%fused_computation.23 | convolution fusion | flops 2161115136 | bytes 7341056 | tf_op jit(solution)/shard_map/dot_general | solution.py:97
  59.2 0.0 collective-permute-done.4
  59.2 0.0 collective-permute-done.5
  59.2 6.0 %fusion.32 = f32[512,1024]{1,0:T(8,128)} fusion(bf16[256,1024]{1,0:T(8,128)(2,1)} %collective-permute-done.9, bf16[256,1024]{1,0:T(8,128)(2,1)} %collective-permute-done.8, bf16[256,1024]{1,0:T(8,128)(2,1)} %collective-permute-done.7, bf16[256,1024]{1,0:T(8,128)(2,1)} %collective-permute-done.6, bf16[1024,256]{1,0:T(8,128)(2,1)} %collective-permute-done.5, ...), kind=kOutput, calls=%fused_computation.35 | convolution fusion | flops 2169503744 | bytes 7341056 | tf_op jit(solution)/shard_map/dot_general | solution.py:97
  65.3 2.3 %fusion.75 = (bf16[128,1024]{1,0:T(8,128)(2,1)S(1)}, bf16[128,1024]{1,0:T(8,128)(2,1)}, bf16[128,1024]{1,0:T(8,128)(2,1)S(1)}) fusion(f32[4,128,1024]{2,1,0:T(8,128)} %bitcast.34, s32[]{:T(128)S(6)} %select_n.91, f32[4,128,1024]{2,1,0:T(8,128)S(1)} %bitcast.32, s32[]{:T(128)S(6)} %select_n.95, s32[]{:T(128)S(6)} %select_n.93), kind=kLoop, calls=%fused_computation.77 | loop fusion | flops 786432 | bytes 3932172 | tf_op jit(solution)/shard_map/convert_element_type | solution.py:125
  67.5 3.6 %collective-permute-start.12 = (bf16[128,1024]{1,0:T(8,128)(2,1)}, bf16[128,1024]{1,0:T(8,128)(2,1)}, u32[]{:S(2)}, u32[]{:S(2)}) collective-permute-start(bf16[128,1024]{1,0:T(8,128)(2,1)} %get-tuple-element.29), channel_id=1, source_target_pairs={{0,3},{1,0},{2,1},{3,2},{4,7},{5,4},{6,5},{7,6},{8,11},{9,8},{10,9... | collective-permute-start | bytes 786440 | tf_op jit(solution)/shard_map/ppermute | solution.py:124
  71.1 0.0 collective-permute-start.11
  71.1 1.0 collective-permute-start.10
  72.2 6.0 %collective-permute-done.12 = bf16[128,1024]{1,0:T(8,128)(2,1)} collective-permute-done((bf16[128,1024]{1,0:T(8,128)(2,1)}, bf16[128,1024]{1,0:T(8,128)(2,1)}, u32[]{:S(2)}, u32[]{:S(2)}) %collective-permute-start.12) | collective-permute-done | bytes 262176 | tf_op jit(solution)/shard_map/ppermute | solution.py:124
  78.2 16.3 %collective-permute-done.11 = bf16[128,1024]{1,0:T(8,128)(2,1)} collective-permute-done((bf16[128,1024]{1,0:T(8,128)(2,1)S(1)}, bf16[128,1024]{1,0:T(8,128)(2,1)}, u32[]{:S(2)}, u32[]{:S(2)}) %collective-permute-start.11) | collective-permute-done | bytes 262176 | tf_op jit(solution)/shard_map/ppermute | solution.py:124
  94.5 1.5 %fusion.72 = bf16[128,1024]{1,0:T(8,128)(2,1)S(1)} fusion(f32[128,1024]{1,0:T(8,128)S(1)} %get-tuple-element.36, bf16[128,1024]{1,0:T(8,128)(2,1)} %collective-permute-done.12, bf16[128,1024]{1,0:T(8,128)(2,1)} %collective-permute-done.11, bf16[128,1024]{1,0:T(8,128)(2,1)} %collective-permute-done.10, f32[4,128,1024]{2,1,0:T(8,128)} %bitcast.35, ...), kind=kLoop, calls=%fused_computation.64 | loop fusion | flops 1179648 | bytes 2621444 | tf_op jit(solution)/shard_map/convert_element_type | solution.py:129
  96.0 14.5 %all_to_all.5 = bf16[16,8,1152]{2,1,0:T(8,128)(2,1)S(1)} all-to-all(bf16[16,8,1152]{2,1,0:T(8,128)(2,1)S(1)} %maximum_bitcast_fusion), channel_id=1, replica_groups=mesh['rep'=2,'member'=4,'tp'=4] {'member','tp'}, dimensions={0} | all-to-all | bytes 589824 | tf_op jit(solution)/shard_map/all_to_all | solution.py:133
  110.5 0.1 convert_reduce_fusion
  110.6 0.3 fusion.66
  111.0 0.9 fusion.41
  (23 shorter events, 0.2 us)
Async XLA Ops:
  7.2 2.0 %copy-start = (bf16[128,1024]{1,0:T(8,128)(2,1)S(1)}, bf16[128,1024]{1,0:T(8,128)(2,1)}, u32[]{:S(2)}) copy-start(bf16[128,1024]{1,0:T(8,128)(2,1)} %param.8) | copy-start | bytes 786436
  7.2 2.4 %copy-start.1 = (f32[2,1024]{1,0:T(2,128)S(1)}, f32[2,1024]{1,0:T(2,128)}, u32[]{:S(2)}) copy-start(f32[2,1024]{1,0:T(2,128)} %param.11) | copy-start | bytes 24580
  7.2 37.5 %all-gather.2.cloned.1.call-start = ((), (), s32[]{:S(2)}) async-start(), calls=%async_computation.1 | async-start | bytes 1474560 | tf_op jit(solution)/shard_map/all_gather | solution.py:83
  10.4 1.3 %copy-start.3 = (bf16[1,1024,512]{2,1,0:T(8,128)(2,1)S(1)}, bf16[1,1024,512]{2,1,0:T(8,128)(2,1)}, u32[]{:S(2)}) copy-start(bf16[1,1024,512]{2,1,0:T(8,128)(2,1)} %param.12) | copy-start | bytes 3145732
  10.4 4.4 %copy-start.2 = (bf16[1,512,1024]{2,1,0:T(8,128)(2,1)S(1)}, bf16[1,512,1024]{2,1,0:T(8,128)(2,1)}, u32[]{:S(2)}) copy-start(bf16[1,512,1024]{2,1,0:T(8,128)(2,1)} %param.13) | copy-start | bytes 3145732
  11.8 15.0 %collective-permute-start.2 = (bf16[1024,256]{1,0:T(8,128)(2,1)S(1)}, bf16[1024,256]{1,0:T(8,128)(2,1)S(1)}, u32[]{:S(2)}, u32[]{:S(2)}) collective-permute-start(bf16[1024,256]{1,0:T(8,128)(2,1)S(1)} %dynamic-slice_bitcast_fusion), channel_id=1, source_target_pairs={{0,8},{4,12},{8,0},{12,4},{1,9},{5,13},{9,1},{13,5},{2,10},{6,14},... | collective-permute-start | bytes 1572872 | tf_op jit(solution)/shard_map/ppermute | solution.py:15
  14.8 30.9 %collective-permute-start.1 = (bf16[512,1024]{1,0:T(8,128)(2,1)S(1)}, bf16[512,1024]{1,0:T(8,128)(2,1)}, u32[]{:S(2)}, u32[]{:S(2)}) collective-permute-start(bf16[512,1024]{1,0:T(8,128)(2,1)S(1)} %bitcast.39), channel_id=1, source_target_pairs={{0,4},{4,0},{8,12},{12,8},{1,5},{5,1},{9,13},{13,9},{2,6},{6,2},{1... | collective-permute-start | bytes 3145736 | tf_op jit(solution)/shard_map/ppermute | solution.py:10
  26.8 13.4 %collective-permute-start.6 = (bf16[256,1024]{1,0:T(8,128)(2,1)S(1)}, bf16[256,1024]{1,0:T(8,128)(2,1)}, u32[]{:S(2)}, u32[]{:S(2)}) collective-permute-start(bf16[256,1024]{1,0:T(8,128)(2,1)S(1)} %constant_dynamic-slice_fusion), channel_id=1, source_target_pairs={{0,8},{4,12},{8,0},{12,4},{1,9},{5,13},{9,1},{13,5},{2,10},{6,14},... | collective-permute-start | bytes 1572872 | tf_op jit(solution)/shard_map/ppermute | solution.py:15
  28.6 25.7 %collective-permute-start = (bf16[1024,512]{1,0:T(8,128)(2,1)S(1)}, bf16[1024,512]{1,0:T(8,128)(2,1)}, u32[]{:S(2)}, u32[]{:S(2)}) collective-permute-start(bf16[1024,512]{1,0:T(8,128)(2,1)S(1)} %bitcast.42), channel_id=1, source_target_pairs={{0,4},{4,0},{8,12},{12,8},{1,5},{5,1},{9,13},{13,9},{2,6},{6,2},{1... | collective-permute-start | bytes 3145736 | tf_op jit(solution)/shard_map/ppermute | solution.py:10
  28.6 17.2 %collective-permute-start.3 = (bf16[1024,256]{1,0:T(8,128)(2,1)S(1)}, bf16[1024,256]{1,0:T(8,128)(2,1)}, u32[]{:S(2)}, u32[]{:S(2)}) collective-permute-start(bf16[1024,256]{1,0:T(8,128)(2,1)S(1)} %collective-permute-done.2), channel_id=1, source_target_pairs={{0,16},{16,0},{1,17},{17,1},{2,18},{18,2},{3,19},{19,3},{4,20},{20... | collective-permute-start | bytes 1572872 | tf_op jit(solution)/shard_map/ppermute | solution.py:21
  40.2 14.1 %collective-permute-start.7 = (bf16[256,1024]{1,0:T(8,128)(2,1)}, bf16[256,1024]{1,0:T(8,128)(2,1)}, u32[]{:S(2)}, u32[]{:S(2)}) collective-permute-start(bf16[256,1024]{1,0:T(8,128)(2,1)} %collective-permute-done.6), channel_id=1, source_target_pairs={{0,16},{16,0},{1,17},{17,1},{2,18},{18,2},{3,19},{19,3},{4,20},{20... | collective-permute-start | bytes 1572872 | tf_op jit(solution)/shard_map/ppermute | solution.py:21
  41.6 17.6 %collective-permute-start.4 = (bf16[1024,256]{1,0:T(8,128)(2,1)S(1)}, bf16[1024,256]{1,0:T(8,128)(2,1)}, u32[]{:S(2)}, u32[]{:S(2)}) collective-permute-start(bf16[1024,256]{1,0:T(8,128)(2,1)S(1)} %collective-permute-done.2), channel_id=1, source_target_pairs={{0,4},{4,0},{8,12},{12,8},{1,5},{5,1},{9,13},{13,9},{2,6},{6,2},{1... | collective-permute-start | bytes 1572872 | tf_op jit(solution)/shard_map/ppermute | solution.py:10
  45.8 13.5 %collective-permute-start.8 = (bf16[256,1024]{1,0:T(8,128)(2,1)}, bf16[256,1024]{1,0:T(8,128)(2,1)}, u32[]{:S(2)}, u32[]{:S(2)}) collective-permute-start(bf16[256,1024]{1,0:T(8,128)(2,1)} %collective-permute-done.6), channel_id=1, source_target_pairs={{0,4},{4,0},{8,12},{12,8},{1,5},{5,1},{9,13},{13,9},{2,6},{6,2},{1... | collective-permute-start | bytes 1572872 | tf_op jit(solution)/shard_map/ppermute | solution.py:10
  45.8 13.4 %collective-permute-start.5 = (bf16[1024,256]{1,0:T(8,128)(2,1)}, bf16[1024,256]{1,0:T(8,128)(2,1)}, u32[]{:S(2)}, u32[]{:S(2)}) collective-permute-start(bf16[1024,256]{1,0:T(8,128)(2,1)} %collective-permute-done.3), channel_id=1, source_target_pairs={{0,4},{4,0},{8,12},{12,8},{1,5},{5,1},{9,13},{13,9},{2,6},{6,2},{1... | collective-permute-start | bytes 1572872 | tf_op jit(solution)/shard_map/ppermute | solution.py:10
  54.3 5.0 %collective-permute-start.9 = (bf16[256,1024]{1,0:T(8,128)(2,1)}, bf16[256,1024]{1,0:T(8,128)(2,1)}, u32[]{:S(2)}, u32[]{:S(2)}) collective-permute-start(bf16[256,1024]{1,0:T(8,128)(2,1)} %collective-permute-done.7), channel_id=1, source_target_pairs={{0,4},{4,0},{8,12},{12,8},{1,5},{5,1},{9,13},{13,9},{2,6},{6,2},{1... | collective-permute-start | bytes 1572872 | tf_op jit(solution)/shard_map/ppermute | solution.py:10
  67.5 10.6 %collective-permute-start.12 = (bf16[128,1024]{1,0:T(8,128)(2,1)}, bf16[128,1024]{1,0:T(8,128)(2,1)}, u32[]{:S(2)}, u32[]{:S(2)}) collective-permute-start(bf16[128,1024]{1,0:T(8,128)(2,1)} %get-tuple-element.29), channel_id=1, source_target_pairs={{0,3},{1,0},{2,1},{3,2},{4,7},{5,4},{6,5},{7,6},{8,11},{9,8},{10,9... | collective-permute-start | bytes 786440 | tf_op jit(solution)/shard_map/ppermute | solution.py:124
  71.1 23.3 %collective-permute-start.11 = (bf16[128,1024]{1,0:T(8,128)(2,1)S(1)}, bf16[128,1024]{1,0:T(8,128)(2,1)}, u32[]{:S(2)}, u32[]{:S(2)}) collective-permute-start(bf16[128,1024]{1,0:T(8,128)(2,1)S(1)} %get-tuple-element.30), channel_id=1, source_target_pairs={{0,2},{1,3},{2,0},{3,1},{4,6},{5,7},{6,4},{7,5},{8,10},{9,11},{10,... | collective-permute-start | bytes 786440 | tf_op jit(solution)/shard_map/ppermute | solution.py:124
  71.1 23.3 %collective-permute-start.10 = (bf16[128,1024]{1,0:T(8,128)(2,1)S(1)}, bf16[128,1024]{1,0:T(8,128)(2,1)}, u32[]{:S(2)}, u32[]{:S(2)}) collective-permute-start(bf16[128,1024]{1,0:T(8,128)(2,1)S(1)} %get-tuple-element.28), channel_id=1, source_target_pairs={{0,1},{1,2},{2,3},{3,0},{4,5},{5,6},{6,7},{7,4},{8,9},{9,10},{10,1... | collective-permute-start | bytes 786440 | tf_op jit(solution)/shard_map/ppermute | solution.py:124
  72.2 38.8 %copy-start.4 = (bf16[1024,128]{1,0:T(8,128)(2,1)S(1)}, bf16[1024,128]{1,0:T(8,128)(2,1)}, u32[]{:S(2)}) copy-start(bf16[1024,128]{1,0:T(8,128)(2,1)} %param.15) | copy-start | bytes 786436
  72.2 38.8 %copy-start.5 = (f32[1024]{0:T(1024)S(1)}, f32[1024]{0:T(1024)}, u32[]{:S(2)}) copy-start(f32[1024]{0:T(1024)} %param.14) | copy-start | bytes 12292
  110.9 1.0 copy-start.6
Sparse Core Ops, SparseCore 0:
  11.5 33.1 all-gather.1
where the time goes:
time: 119 us
  waiting for transfers between devices  55.4 us (47%)
  blocking collectives  14.5 us (12%)
  between operations  14.3 us (12%)
  starting transfers between devices  12.9 us (11%)
  matrix products  12.5 us (11%)
  other arithmetic  7.9 us (7%)
  local copies, waits for them, and re-layouts  1.27 us (1%)
    ppermute x3, waiting for transfers between devices, local(): lax.ppermute(slice_for((tp_here + shift) % n_tp).astype(PARTIAL_DTYPE), '...  22.3 us
    ppermute x2, waiting for transfers between devices, from_chip_behind(): lax.ppermute(value, axis, [(i, (i + 2 * chips_back) % size) for i in rang...  22 us
    all_to_all x1, blocking collectives, local(): lax.all_to_all(jnp.concatenate([packed, spot_lanes], axis=1).reshape(n_de...  14.5 us
    dot_general x2, matrix products, apply_block(): return jnp.dot(hidden, down_here, preferred_element_type=jnp.float32)  10.9 us
    ppermute x2, waiting for transfers between devices, swap_parts(): lax.ppermute(value, 'rep', [(i, (i + step) % n_rep) for i in range(n_rep)])  7.94 us
    ppermute x2, starting transfers between devices, from_chip_behind(): lax.ppermute(value, axis, [(i, (i + 2 * chips_back) % size) for i in rang...  4.84 us
    ppermute x3, starting transfers between devices, local(): lax.ppermute(slice_for((tp_here + shift) % n_tp).astype(PARTIAL_DTYPE), '...  4.61 us
    all_gather x1, waiting for transfers between devices, local(): lax.all_gather(jnp.concatenate([normed, member_lanes], axis=1), 'tp', axi...  3.1 us
  transfers between devices with their start and end apart: 14, of which 6 were waited for; matrix products, arithmetic and copies ran while one was open for 5% of the time, Pallas kernels for 0%

commit v1 on v0

--- a/solution.py
+++ b/solution.py
@@ -4,6 +4,18 @@
 from jax.sharding import PartitionSpec as P
 
 PARTIAL_DTYPE = jnp.bfloat16
+
+
+def collect(x, axis, dim):
+    ways, here, step = (lax.axis_size(axis), lax.axis_index(axis), x.shape[dim])
+    line, have = (x, 1)
+    while have < ways:
+        line = jnp.concatenate(
+            [line, lax.ppermute(line, axis, [(d, (d - have) % ways) for d in range(ways)])],
+            axis=dim,
+        )
+        have = 2 * have
+    return jnp.roll(line, here * step, axis=dim)
 
 
 def from_partner(value, axis, distance):
@@ -80,9 +92,7 @@
     member_lanes = jnp.where(
         jnp.arange(128, dtype=jnp.int32)[None, :] == 0, member[:, None], 0
     ).astype(jnp.bfloat16)
-    gathered = lax.all_gather(
-        jnp.concatenate([normed, member_lanes], axis=1), "tp", axis=0, tiled=True
-    )
+    gathered = collect(jnp.concatenate([normed, member_lanes], axis=1), "tp", 0)
     gathered_rows = gathered[:, :feature_width]
     gathered_member = gathered[:, feature_width].astype(jnp.int32)
 

time: 119 us -> 117 us (0.983)
  between operations: 14.3 us -> 0.86 us
  local copies, waits for them, and re-layouts: 1.27 us -> 7.01 us
  starting transfers between devices: 12.9 us -> 16.8 us
  blocking collectives: 14.5 us -> 16.1 us
    ppermute x0 -> x2, waiting for transfers between devices: none -> 17 us  [collect(): lax.ppermute(line, axis, [(d, (d - have) % ways) for d in range(ways)])]
    ppermute x2, waiting for transfers between devices: 22 us -> 6.68 us  [from_chip_behind(): lax.ppermute(value, axis, [(i, (i + 2 * chips_back) % size) for i in rang...]
    ppermute x0 -> x2, starting transfers between devices: none -> 6.59 us  [collect(): lax.ppermute(line, axis, [(d, (d - have) % ways) for d in range(ways)])]
    all_gather x1 -> x0, waiting for transfers between devices: 3.1 us -> none  [local(): lax.all_gather(jnp.concatenate([normed, member_lanes], axis=1), 'tp', axi...]
    unnamed x14 -> x17, local copies, waits for them, and re-layouts: 0.42 us -> 3.19 us
    ppermute x3, starting transfers between devices: 4.61 us -> 2.92 us  [local(): lax.ppermute(slice_for((tp_here + shift) % n_tp).astype(PARTIAL_DTYPE), '...]
    ppermute x2, starting transfers between devices: 4.84 us -> 3.17 us  [from_chip_behind(): lax.ppermute(value, axis, [(i, (i + 2 * chips_back) % size) for i in rang...]
    all_to_all x1, blocking collectives: 14.5 us -> 16.1 us  [local(): lax.all_to_all(jnp.concatenate([packed, spot_lanes], axis=1).reshape(n_de...]
  transfers between devices with their start and end apart: 14 -> 15, of which waited for: 6 -> 6; matrix products, arithmetic and copies ran while one was open for 5% -> 11% of each run, Pallas kernels for 0% -> 0%
where the time goes in v1:
time: 117 us
  waiting for transfers between devices  54.7 us (47%)
  starting transfers between devices  16.8 us (14%)
  blocking collectives  16.1 us (14%)
  matrix products  12.5 us (11%)
  other arithmetic  8.72 us (7%)
  local copies, waits for them, and re-layouts  7.01 us (6%)
    ppermute x3, waiting for transfers between devices, local(): lax.ppermute(slice_for((tp_here + shift) % n_tp).astype(PARTIAL_DTYPE), '...  22 us
    ppermute x2, waiting for transfers between devices, collect(): lax.ppermute(line, axis, [(d, (d - have) % ways) for d in range(ways)])  17 us
    all_to_all x1, blocking collectives, local(): lax.all_to_all(jnp.concatenate([packed, spot_lanes], axis=1).reshape(n_de...  16.1 us
    dot_general x2, matrix products, apply_block(): return jnp.dot(hidden, down_here, preferred_element_type=jnp.float32)  11 us
    ppermute x2, waiting for transfers between devices, swap_parts(): lax.ppermute(value, 'rep', [(i, (i + step) % n_rep) for i in range(n_rep)])  9.1 us
    ppermute x2, waiting for transfers between devices, from_chip_behind(): lax.ppermute(value, axis, [(i, (i + 2 * chips_back) % size) for i in rang...  6.68 us
    ppermute x2, starting transfers between devices, collect(): lax.ppermute(line, axis, [(d, (d - have) % ways) for d in range(ways)])  6.59 us
    unnamed x17, local copies, waits for them, and re-layouts  3.19 us
  transfers between devices with their start and end apart: 15, of which 6 were waited for; matrix products, arithmetic and copies ran while one was open for 11% of the time, Pallas kernels for 0%

profile of v1, /device:TPU:0, one launch (start us, length us, event | category | flops | bytes accessed | tf_op | source)
XLA Modules:
  0.0 116.7 jit_solution(2876991393173257868)
XLA Ops:
  0.6 0.0 copy-start
  0.7 0.7 and_select_fusion
  1.4 0.1 fusion.86
  1.5 0.2 reduce_window_sum.11
  1.6 0.2 select_reduce_fusion.2
  1.8 0.8 select_reduce_fusion.1
  2.6 0.3 multiply_reduce_fusion
  2.9 0.1 select_convert_fusion.1
  3.1 0.8 gather_fusion
  3.8 0.1 multiply_convert_fusion
  4.0 0.8 pad_maximum_fusion.1
  4.7 5.1 %collective-permute-start = (bf16[128,1152]{1,0:T(8,128)(2,1)S(1)}, bf16[128,1152]{1,0:T(8,128)(2,1)S(1)}, u32[]{:S(2)}, u32[]{:S(2)}) collective-permute-start(bf16[128,1152]{1,0:T(8,128)(2,1)S(1)} %get-tuple-element.31), channel_id=1, source_target_pairs={{0,3},{1,0},{2,1},{3,2},{4,7},{5,4},{6,5},{7,6},{8,11},{9,8},{10,9... | collective-permute-start | bytes 884744 | tf_op jit(solution)/shard_map/ppermute | solution.py:14
  9.8 1.1 dynamic-slice_bitcast_fusion
  10.9 1.6 %collective-permute-start.4 = (bf16[1024,256]{1,0:T(8,128)(2,1)S(1)}, bf16[1024,256]{1,0:T(8,128)(2,1)S(1)}, u32[]{:S(2)}, u32[]{:S(2)}) collective-permute-start(bf16[1024,256]{1,0:T(8,128)(2,1)S(1)} %dynamic-slice_bitcast_fusion), channel_id=1, source_target_pairs={{0,8},{4,12},{8,0},{12,4},{1,9},{5,13},{9,1},{13,5},{2,10},{6,14},... | collective-permute-start | bytes 1572872 | tf_op jit(solution)/shard_map/ppermute | solution.py:27
  12.5 3.6 %collective-permute-done = bf16[128,1152]{1,0:T(8,128)(2,1)S(1)} collective-permute-done((bf16[128,1152]{1,0:T(8,128)(2,1)S(1)}, bf16[128,1152]{1,0:T(8,128)(2,1)S(1)}, u32[]{:S(2)}, u32[]{:S(2)}) %collective-permute-start) | collective-permute-done | bytes 294944 | tf_op jit(solution)/shard_map/ppermute | solution.py:14
  16.1 1.5 %collective-permute-start.1 = (bf16[256,1152]{1,0:T(8,128)(2,1)S(1)}, bf16[256,1152]{1,0:T(8,128)(2,1)S(1)}, u32[]{:S(2)}, u32[]{:S(2)}) collective-permute-start(bf16[256,1152]{1,0:T(8,128)(2,1)S(1)} %pad_maximum_fusion), channel_id=1, source_target_pairs={{0,2},{1,3},{2,0},{3,1},{4,6},{5,7},{6,4},{7,5},{8,10},{9,11},{10,... | collective-permute-start | bytes 1769480 | tf_op jit(solution)/shard_map/ppermute | solution.py:14
  17.6 6.7 %collective-permute-done.4 = bf16[1024,256]{1,0:T(8,128)(2,1)S(1)} collective-permute-done((bf16[1024,256]{1,0:T(8,128)(2,1)S(1)}, bf16[1024,256]{1,0:T(8,128)(2,1)S(1)}, u32[]{:S(2)}, u32[]{:S(2)}) %collective-permute-start.4) | collective-permute-done | bytes 524320 | tf_op jit(solution)/shard_map/ppermute | solution.py:27
  24.3 0.8 copy-done.2
  25.1 1.1 constant_dynamic-slice_fusion
  26.2 1.6 %collective-permute-start.8 = (bf16[256,1024]{1,0:T(8,128)(2,1)S(1)}, bf16[256,1024]{1,0:T(8,128)(2,1)}, u32[]{:S(2)}, u32[]{:S(2)}) collective-permute-start(bf16[256,1024]{1,0:T(8,128)(2,1)S(1)} %constant_dynamic-slice_fusion), channel_id=1, source_target_pairs={{0,8},{4,12},{8,0},{12,4},{1,9},{5,13},{9,1},{13,5},{2,10},{6,14},... | collective-permute-start | bytes 1572872 | tf_op jit(solution)/shard_map/ppermute | solution.py:27
  27.8 0.5 collective-permute-start.2
  28.3 0.7 constant_dynamic-update-slice_fusion.4
  29.0 1.5 %collective-permute-start.5 = (bf16[1024,256]{1,0:T(8,128)(2,1)}, bf16[1024,256]{1,0:T(8,128)(2,1)}, u32[]{:S(2)}, u32[]{:S(2)}) collective-permute-start(bf16[1024,256]{1,0:T(8,128)(2,1)} %copy-done.2), channel_id=1, source_target_pairs={{0,16},{16,0},{1,17},{17,1},{2,18},{18,2},{3,19},{19,3},{4,20},{20... | collective-permute-start | bytes 1572872 | tf_op jit(solution)/shard_map/ppermute | solution.py:33
  30.5 13.4 %collective-permute-done.1 = bf16[256,1152]{1,0:T(8,128)(2,1)S(1)} collective-permute-done((bf16[256,1152]{1,0:T(8,128)(2,1)S(1)}, bf16[256,1152]{1,0:T(8,128)(2,1)S(1)}, u32[]{:S(2)}, u32[]{:S(2)}) %collective-permute-start.1) | collective-permute-done | bytes 589856 | tf_op jit(solution)/shard_map/ppermute | solution.py:14
  43.9 0.9 constant_dynamic-update-slice_fusion.3
  44.8 1.5 %collective-permute-start.9 = (bf16[256,1024]{1,0:T(8,128)(2,1)}, bf16[256,1024]{1,0:T(8,128)(2,1)}, u32[]{:S(2)}, u32[]{:S(2)}) collective-permute-start(bf16[256,1024]{1,0:T(8,128)(2,1)} %collective-permute-done.8), channel_id=1, source_target_pairs={{0,16},{16,0},{1,17},{17,1},{2,18},{18,2},{3,19},{19,3},{4,20},{20... | collective-permute-start | bytes 1572872 | tf_op jit(solution)/shard_map/ppermute | solution.py:33
  46.3 0.8 constant_dynamic-update-slice_fusion.2
  47.0 0.7 constant_dynamic-update-slice_fusion.1
  47.8 0.9 constant_dynamic-update-slice_fusion
  48.7 1.1 fusion.84
  49.8 0.0 collective-permute-done.3
  49.8 0.3 collective-permute-start.10
  50.1 0.0 collective-permute-done.5
  50.1 0.3 collective-permute-start.7
  50.3 9.1 %collective-permute-done.9 = bf16[256,1024]{1,0:T(8,128)(2,1)} collective-permute-done((bf16[256,1024]{1,0:T(8,128)(2,1)}, bf16[256,1024]{1,0:T(8,128)(2,1)}, u32[]{:S(2)}, u32[]{:S(2)}) %collective-permute-start.9) | collective-permute-done | bytes 524320 | tf_op jit(solution)/shard_map/ppermute | solution.py:33
  59.4 0.0 collective-permute-start.11
  59.5 5.0 %fusion.20 = f32[512,1024]{1,0:T(8,128)S(1)} fusion(bf16[512,1024]{1,0:T(8,128)(2,1)} %collective-permute-done.3, bf16[512,1024]{1,0:T(8,128)(2,1)} %bitcast.40, bf16[1024,512]{1,0:T(8,128)(2,1)} %collective-permute-done.2, bf16[1024,512]{1,0:T(8,128)(2,1)} %bitcast.42, bf16[1024,1152]{1,0:T(8,128)(2,1)} %constant_dynamic-update-slice_fusion, ...), kind=kOutput, calls=%fused_computation.23 | convolution fusion | flops 2161115136 | bytes 7341060 | tf_op jit(solution)/shard_map/dot_general | solution.py:107
  64.5 6.0 %fusion.32 = f32[512,1024]{1,0:T(8,128)} fusion(bf16[256,1024]{1,0:T(8,128)(2,1)} %collective-permute-done.11, bf16[256,1024]{1,0:T(8,128)(2,1)} %collective-permute-done.10, bf16[256,1024]{1,0:T(8,128)(2,1)} %collective-permute-done.9, bf16[256,1024]{1,0:T(8,128)(2,1)} %collective-permute-done.8, bf16[512]{0:T(512)(128)(2,1)S(1)} %get-tuple-element.24, ...), kind=kOutput, calls=%fused_computation.35 | convolution fusion | flops 2169503744 | bytes 7341060 | tf_op jit(solution)/shard_map/dot_general | solution.py:107
  70.5 2.3 %fusion.75 = (bf16[128,1024]{1,0:T(8,128)(2,1)S(1)}, bf16[128,1024]{1,0:T(8,128)(2,1)}, bf16[128,1024]{1,0:T(8,128)(2,1)S(1)}) fusion(f32[4,128,1024]{2,1,0:T(8,128)} %bitcast.34, s32[]{:T(128)S(6)} %select_n.105, f32[4,128,1024]{2,1,0:T(8,128)S(1)} %bitcast.32, s32[]{:T(128)S(6)} %select_n.109, s32[]{:T(128)S(6)} %select_n.107), kind=kLoop, calls=%fused_computation.78 | loop fusion | flops 786432 | bytes 3932172 | tf_op jit(solution)/shard_map/convert_element_type | solution.py:135
  72.8 2.4 %collective-permute-start.14 = (bf16[128,1024]{1,0:T(8,128)(2,1)}, bf16[128,1024]{1,0:T(8,128)(2,1)}, u32[]{:S(2)}, u32[]{:S(2)}) collective-permute-start(bf16[128,1024]{1,0:T(8,128)(2,1)} %get-tuple-element.29), channel_id=1, source_target_pairs={{0,3},{1,0},{2,1},{3,2},{4,7},{5,4},{6,5},{7,6},{8,11},{9,8},{10,9... | collective-permute-start | bytes 786440 | tf_op jit(solution)/shard_map/ppermute | solution.py:134
  75.1 0.6 collective-permute-start.12
  75.7 7.8 %collective-permute-done.14 = bf16[128,1024]{1,0:T(8,128)(2,1)} collective-permute-done((bf16[128,1024]{1,0:T(8,128)(2,1)}, bf16[128,1024]{1,0:T(8,128)(2,1)}, u32[]{:S(2)}, u32[]{:S(2)}) %collective-permute-start.14) | collective-permute-done | bytes 262176 | tf_op jit(solution)/shard_map/ppermute | solution.py:134
  83.5 14.2 %collective-permute-done.13 = bf16[128,1024]{1,0:T(8,128)(2,1)} collective-permute-done((bf16[128,1024]{1,0:T(8,128)(2,1)S(1)}, bf16[128,1024]{1,0:T(8,128)(2,1)}, u32[]{:S(2)}, u32[]{:S(2)}) %collective-permute-start.13) | collective-permute-done | bytes 262176 | tf_op jit(solution)/shard_map/ppermute | solution.py:134
  97.7 1.5 %fusion.64 = bf16[128,1024]{1,0:T(8,128)(2,1)S(1)} fusion(f32[128,1024]{1,0:T(8,128)S(1)} %get-tuple-element.38, bf16[128,1024]{1,0:T(8,128)(2,1)} %collective-permute-done.14, bf16[128,1024]{1,0:T(8,128)(2,1)} %collective-permute-done.13, bf16[128,1024]{1,0:T(8,128)(2,1)} %collective-permute-done.12, f32[4,128,1024]{2,1,0:T(8,128)} %bitcast.35, ...), kind=kLoop, calls=%fused_computation.65 | loop fusion | flops 1179648 | bytes 2621444 | tf_op jit(solution)/shard_map/convert_element_type | solution.py:139
  99.2 16.1 %all_to_all.5 = bf16[16,8,1152]{2,1,0:T(8,128)(2,1)S(1)} all-to-all(bf16[16,8,1152]{2,1,0:T(8,128)(2,1)S(1)} %maximum_bitcast_fusion), channel_id=1, replica_groups=mesh['rep'=2,'member'=4,'tp'=4] {'member','tp'}, dimensions={0} | all-to-all | bytes 589824 | tf_op jit(solution)/shard_map/all_to_all | solution.py:143
  115.3 0.1 convert_reduce_fusion
  115.4 0.3 fusion.58
  115.8 0.9 fusion.41
  (30 shorter events, 0.2 us)
Async XLA Ops:
  0.6 2.0 %copy-start = (bf16[128,1024]{1,0:T(8,128)(2,1)S(1)}, bf16[128,1024]{1,0:T(8,128)(2,1)}, u32[]{:S(2)}) copy-start(bf16[128,1024]{1,0:T(8,128)(2,1)} %param.8) | copy-start | bytes 786436
  0.6 2.4 %copy-start.1 = (f32[2,1024]{1,0:T(2,128)S(1)}, f32[2,1024]{1,0:T(2,128)}, u32[]{:S(2)}) copy-start(f32[2,1024]{1,0:T(2,128)} %param.11) | copy-start | bytes 24580
  4.7 11.3 %collective-permute-start = (bf16[128,1152]{1,0:T(8,128)(2,1)S(1)}, bf16[128,1152]{1,0:T(8,128)(2,1)S(1)}, u32[]{:S(2)}, u32[]{:S(2)}) collective-permute-start(bf16[128,1152]{1,0:T(8,128)(2,1)S(1)} %get-tuple-element.31), channel_id=1, source_target_pairs={{0,3},{1,0},{2,1},{3,2},{4,7},{5,4},{6,5},{7,6},{8,11},{9,8},{10,9... | collective-permute-start | bytes 884744 | tf_op jit(solution)/shard_map/ppermute | solution.py:14
  10.9 13.4 %collective-permute-start.4 = (bf16[1024,256]{1,0:T(8,128)(2,1)S(1)}, bf16[1024,256]{1,0:T(8,128)(2,1)S(1)}, u32[]{:S(2)}, u32[]{:S(2)}) collective-permute-start(bf16[1024,256]{1,0:T(8,128)(2,1)S(1)} %dynamic-slice_bitcast_fusion), channel_id=1, source_target_pairs={{0,8},{4,12},{8,0},{12,4},{1,9},{5,13},{9,1},{13,5},{2,10},{6,14},... | collective-permute-start | bytes 1572872 | tf_op jit(solution)/shard_map/ppermute | solution.py:27
  16.1 27.8 %collective-permute-start.1 = (bf16[256,1152]{1,0:T(8,128)(2,1)S(1)}, bf16[256,1152]{1,0:T(8,128)(2,1)S(1)}, u32[]{:S(2)}, u32[]{:S(2)}) collective-permute-start(bf16[256,1152]{1,0:T(8,128)(2,1)S(1)} %pad_maximum_fusion), channel_id=1, source_target_pairs={{0,2},{1,3},{2,0},{3,1},{4,6},{5,7},{6,4},{7,5},{8,10},{9,11},{10,... | collective-permute-start | bytes 1769480 | tf_op jit(solution)/shard_map/ppermute | solution.py:14
  24.3 0.8 copy-start.2
  26.2 18.6 %collective-permute-start.8 = (bf16[256,1024]{1,0:T(8,128)(2,1)S(1)}, bf16[256,1024]{1,0:T(8,128)(2,1)}, u32[]{:S(2)}, u32[]{:S(2)}) collective-permute-start(bf16[256,1024]{1,0:T(8,128)(2,1)S(1)} %constant_dynamic-slice_fusion), channel_id=1, source_target_pairs={{0,8},{4,12},{8,0},{12,4},{1,9},{5,13},{9,1},{13,5},{2,10},{6,14},... | collective-permute-start | bytes 1572872 | tf_op jit(solution)/shard_map/ppermute | solution.py:27
  27.8 22.0 %collective-permute-start.3 = (bf16[512,1024]{1,0:T(8,128)(2,1)}, bf16[512,1024]{1,0:T(8,128)(2,1)}, u32[]{:S(2)}, u32[]{:S(2)}) collective-permute-start(bf16[512,1024]{1,0:T(8,128)(2,1)} %bitcast.39), channel_id=1, source_target_pairs={{0,4},{4,0},{8,12},{12,8},{1,5},{5,1},{9,13},{13,9},{2,6},{6,2},{1... | collective-permute-start | bytes 3145736 | tf_op jit(solution)/shard_map/ppermute | solution.py:22
  27.8 31.7 %collective-permute-start.2 = (bf16[1024,512]{1,0:T(8,128)(2,1)}, bf16[1024,512]{1,0:T(8,128)(2,1)}, u32[]{:S(2)}, u32[]{:S(2)}) collective-permute-start(bf16[1024,512]{1,0:T(8,128)(2,1)} %bitcast.41), channel_id=1, source_target_pairs={{0,4},{4,0},{8,12},{12,8},{1,5},{5,1},{9,13},{13,9},{2,6},{6,2},{1... | collective-permute-start | bytes 3145736 | tf_op jit(solution)/shard_map/ppermute | solution.py:22
  29.0 21.0 %collective-permute-start.5 = (bf16[1024,256]{1,0:T(8,128)(2,1)}, bf16[1024,256]{1,0:T(8,128)(2,1)}, u32[]{:S(2)}, u32[]{:S(2)}) collective-permute-start(bf16[1024,256]{1,0:T(8,128)(2,1)} %copy-done.2), channel_id=1, source_target_pairs={{0,16},{16,0},{1,17},{17,1},{2,18},{18,2},{3,19},{19,3},{4,20},{20... | collective-permute-start | bytes 1572872 | tf_op jit(solution)/shard_map/ppermute | solution.py:33
  43.9 20.5 %collective-permute-start.6 = (bf16[1024,256]{1,0:T(8,128)(2,1)}, bf16[1024,256]{1,0:T(8,128)(2,1)}, u32[]{:S(2)}, u32[]{:S(2)}) collective-permute-start(bf16[1024,256]{1,0:T(8,128)(2,1)} %copy-done.2), channel_id=1, source_target_pairs={{0,4},{4,0},{8,12},{12,8},{1,5},{5,1},{9,13},{13,9},{2,6},{6,2},{1... | collective-permute-start | bytes 1572872 | tf_op jit(solution)/shard_map/ppermute | solution.py:22
  44.8 14.7 %collective-permute-start.9 = (bf16[256,1024]{1,0:T(8,128)(2,1)}, bf16[256,1024]{1,0:T(8,128)(2,1)}, u32[]{:S(2)}, u32[]{:S(2)}) collective-permute-start(bf16[256,1024]{1,0:T(8,128)(2,1)} %collective-permute-done.8), channel_id=1, source_target_pairs={{0,16},{16,0},{1,17},{17,1},{2,18},{18,2},{3,19},{19,3},{4,20},{20... | collective-permute-start | bytes 1572872 | tf_op jit(solution)/shard_map/ppermute | solution.py:33
  49.8 14.7 %collective-permute-start.10 = (bf16[256,1024]{1,0:T(8,128)(2,1)}, bf16[256,1024]{1,0:T(8,128)(2,1)}, u32[]{:S(2)}, u32[]{:S(2)}) collective-permute-start(bf16[256,1024]{1,0:T(8,128)(2,1)} %collective-permute-done.8), channel_id=1, source_target_pairs={{0,4},{4,0},{8,12},{12,8},{1,5},{5,1},{9,13},{13,9},{2,6},{6,2},{1... | collective-permute-start | bytes 1572872 | tf_op jit(solution)/shard_map/ppermute | solution.py:22
  50.1 14.4 %collective-permute-start.7 = (bf16[1024,256]{1,0:T(8,128)(2,1)}, bf16[1024,256]{1,0:T(8,128)(2,1)}, u32[]{:S(2)}, u32[]{:S(2)}) collective-permute-start(bf16[1024,256]{1,0:T(8,128)(2,1)} %collective-permute-done.5), channel_id=1, source_target_pairs={{0,4},{4,0},{8,12},{12,8},{1,5},{5,1},{9,13},{13,9},{2,6},{6,2},{1... | collective-permute-start | bytes 1572872 | tf_op jit(solution)/shard_map/ppermute | solution.py:22
  59.4 5.0 %collective-permute-start.11 = (bf16[256,1024]{1,0:T(8,128)(2,1)}, bf16[256,1024]{1,0:T(8,128)(2,1)}, u32[]{:S(2)}, u32[]{:S(2)}) collective-permute-start(bf16[256,1024]{1,0:T(8,128)(2,1)} %collective-permute-done.9), channel_id=1, source_target_pairs={{0,4},{4,0},{8,12},{12,8},{1,5},{5,1},{9,13},{13,9},{2,6},{6,2},{1... | collective-permute-start | bytes 1572872 | tf_op jit(solution)/shard_map/ppermute | solution.py:22
  59.4 5.0 %copy-start.3 = (bf16[1024,256]{1,0:T(8,128)(2,1)S(1)}, bf16[1024,256]{1,0:T(8,128)(2,1)}, u32[]{:S(2)}) copy-start(bf16[1024,256]{1,0:T(8,128)(2,1)} %copy-done.2) | copy-start | bytes 1572868
  72.8 10.7 %collective-permute-start.14 = (bf16[128,1024]{1,0:T(8,128)(2,1)}, bf16[128,1024]{1,0:T(8,128)(2,1)}, u32[]{:S(2)}, u32[]{:S(2)}) collective-permute-start(bf16[128,1024]{1,0:T(8,128)(2,1)} %get-tuple-element.29), channel_id=1, source_target_pairs={{0,3},{1,0},{2,1},{3,2},{4,7},{5,4},{6,5},{7,6},{8,11},{9,8},{10,9... | collective-permute-start | bytes 786440 | tf_op jit(solution)/shard_map/ppermute | solution.py:134
  75.1 22.5 %collective-permute-start.13 = (bf16[128,1024]{1,0:T(8,128)(2,1)S(1)}, bf16[128,1024]{1,0:T(8,128)(2,1)}, u32[]{:S(2)}, u32[]{:S(2)}) collective-permute-start(bf16[128,1024]{1,0:T(8,128)(2,1)S(1)} %get-tuple-element.30), channel_id=1, source_target_pairs={{0,2},{1,3},{2,0},{3,1},{4,6},{5,7},{6,4},{7,5},{8,10},{9,11},{10,... | collective-permute-start | bytes 786440 | tf_op jit(solution)/shard_map/ppermute | solution.py:134
  75.1 22.5 %collective-permute-start.12 = (bf16[128,1024]{1,0:T(8,128)(2,1)S(1)}, bf16[128,1024]{1,0:T(8,128)(2,1)}, u32[]{:S(2)}, u32[]{:S(2)}) collective-permute-start(bf16[128,1024]{1,0:T(8,128)(2,1)S(1)} %get-tuple-element.28), channel_id=1, source_target_pairs={{0,1},{1,2},{2,3},{3,0},{4,5},{5,6},{6,7},{7,4},{8,9},{9,10},{10,1... | collective-permute-start | bytes 786440 | tf_op jit(solution)/shard_map/ppermute | solution.py:134
  75.7 40.1 %copy-start.4 = (bf16[1024,128]{1,0:T(8,128)(2,1)S(1)}, bf16[1024,128]{1,0:T(8,128)(2,1)}, u32[]{:S(2)}) copy-start(bf16[1024,128]{1,0:T(8,128)(2,1)} %param.15) | copy-start | bytes 786436
  75.7 40.1 %copy-start.5 = (f32[1024]{0:T(1024)S(1)}, f32[1024]{0:T(1024)}, u32[]{:S(2)}) copy-start(f32[1024]{0:T(1024)} %param.14) | copy-start | bytes 12292
  115.8 1.0 copy-start.6
